TPU v7x, 256 devices: a whole 4x4x8 slice. The times are simulated.
256 devices in a mesh: gx: 8 (over x, core), gy: 32 (over y, z).
Axes of the slice: x: 4, y: 4, z: 8, core: 2. Of those that a mesh axis runs over, the one named last changes fastest.
Arguments:
- hidden_in: bfloat16 [8192, 4096], P('gx', 'gy')
- norm_gain: bfloat16 [4096], P('gy'), may hold values from 0.099609375 to 1.8984375
- query_proj: bfloat16 [4096, 4096], P('gx', 'gy')
- kv_proj: bfloat16 [1024, 4096], P(None, 'gy')
- prompt_lengths: int32 [8], replicated, may hold values from 1 to 4096, 8192 in all
- cache_slot: int32 [512], replicated, may hold values from 0 to 511, as said below
Outputs:
- attention: bfloat16 [8192, 4096], P('gy', 'gx')
- kv_cache: bfloat16 [512, 16, 1024], P('gy', None, 'gx')
Inputs may be any that keep to these rules, and one draw needn't show every extreme that they name: `prompt_lengths`: the 8 prompts sum to 8192 tokens; the longest has exactly 4096. `cache_slot`: A permutation of the 512 slots; slot s is held by index s // 16 of gy. The 16 pages of one token block go to any one index at most 1 times, and every index receives exactly 16 pages.
All inputs are finite; a program needn't handle non-finite values.
Results may differ from a plain program's by a relative error of at most 0.0066.
The roundings to bfloat16 on the way count: a program that leaves them out, or rounds other values in their place, can miss the bound.
Values may be sent and summed in bfloat16 or wider, within the bound.
No kernel may reach another device: no remote copies, remote signals or barrier semaphores. Data moves between devices by JAX's collectives and lax.ppermute only.
A program may use at most 128 MiB of HBM per device.

v0:
```python
import math
import jax
import jax.numpy as jnp
from jax import lax
from jax.sharding import PartitionSpec as P

D = 4096
H = 32
KVH = 4
HD = 128
PAGES_DEV = 16
MOST = 4096
epsilon = 1e-06
rope_base = 5000000.0
masked_out = -1e30


def token_places(prompt_lengths, token_index):
    prompt_ends = jnp.cumsum(prompt_lengths)
    prompt_starts = prompt_ends - prompt_lengths
    segment = jnp.sum((token_index[:, None] >= prompt_ends[None, :]).astype(jnp.int32), axis=1)
    chosen = segment[:, None] == jnp.arange(prompt_lengths.shape[0], dtype=jnp.int32)[None, :]
    opening = jnp.sum(jnp.where(chosen, prompt_starts[None, :], 0), axis=1)
    return (segment, token_index - opening)


def rotate(vectors, places):
    half_size = vectors.shape[-1] // 2
    frequency = rope_base ** (-(jnp.arange(half_size, dtype=jnp.float32) * 2.0) / vectors.shape[-1])
    angles = places.astype(jnp.float32)[:, None] * frequency[None, :]
    cos_part = jnp.cos(angles)[:, None, :]
    sin_part = jnp.sin(angles)[:, None, :]
    leading = vectors[..., :half_size]
    trailing = vectors[..., half_size:]
    return jnp.concatenate(
        [leading * cos_part - trailing * sin_part, trailing * cos_part + leading * sin_part],
        axis=-1,
    )


def local(hidden_in, norm_gain, query_proj, kv_proj, prompt_lengths, cache_slot):
    count_gx = lax.axis_size("gx")
    count_gy = lax.axis_size("gy")
    where_gx = lax.axis_index("gx")
    where_gy = lax.axis_index("gy")
    local_rows, local_feats = hidden_in.shape
    features = local_feats * count_gy
    block_tokens = local_rows * count_gx // count_gy
    all_tokens = block_tokens * count_gy
    blocks_per_slab = local_rows // block_tokens
    sub = block_tokens // count_gy
    heads_here = query_proj.shape[0] // HD
    query_cols = heads_here * HD
    is_key = where_gx % 2 == 0
    kv_rows = lax.dynamic_slice_in_dim(kv_proj, where_gx * HD, HD, 0)
    stacked = jnp.concatenate([query_proj, kv_rows], axis=0)
    weights_full = lax.all_gather(stacked, "gy", axis=1, tiled=True)
    gain_full = lax.all_gather(norm_gain, "gy", axis=0, tiled=True)
    pieces = hidden_in.reshape(blocks_per_slab, count_gy, sub, local_feats)
    pieces = lax.all_to_all(pieces, "gy", 1, 1, tiled=True)
    rows_here = lax.all_gather(pieces, "gx", axis=0, tiled=False)
    rows_here = rows_here.transpose(0, 1, 3, 2, 4).reshape(block_tokens, features)
    widened = rows_here.astype(jnp.float32)
    squares = jnp.sum(widened * widened, axis=1)
    normed = (
        widened
        * lax.rsqrt(squares / features + epsilon)[:, None]
        * gain_full.astype(jnp.float32)[None, :]
    ).astype(jnp.bfloat16)
    contract = (((1,), (1,)), ((), ()))
    projected = lax.dot_general(normed, weights_full, contract, preferred_element_type=jnp.float32)
    order = jnp.arange(block_tokens, dtype=jnp.int32)
    my_tokens = order // sub * block_tokens + where_gy * sub + order % sub
    unused_segment, my_places = token_places(prompt_lengths, my_tokens)
    queries = rotate(
        projected[:, :query_cols].reshape(block_tokens, heads_here, HD), my_places
    ).astype(jnp.bfloat16)
    half_raw = projected[:, query_cols:]
    rotated = rotate(half_raw[:, None, :], my_places)[:, 0, :]
    mine = jnp.where(is_key, rotated, half_raw).astype(jnp.bfloat16)
    queries = lax.all_to_all(
        queries.reshape(count_gy, sub, query_cols), "gy", 0, 0, tiled=True
    ).reshape(block_tokens, heads_here, HD)
    mine_all = lax.all_gather(mine.reshape(count_gy, sub, HD), "gy", axis=0, tiled=False)
    mine_all = mine_all.transpose(1, 0, 2, 3).reshape(all_tokens, HD)
    other_all = lax.ppermute(mine_all, "gx", [(p, p ^ 1) for p in range(count_gx)])
    keys = jnp.where(is_key, mine_all, other_all)
    values = jnp.where(is_key, other_all, mine_all)
    every_index = jnp.arange(all_tokens, dtype=jnp.int32)
    segment_all, unused_places = token_places(prompt_lengths, every_index)
    first_query = where_gy * block_tokens
    token_index = first_query + order
    segment_own = lax.dynamic_slice_in_dim(segment_all, first_query, block_tokens, 0)
    window_blocks = min(count_gy, MOST // block_tokens + 1)
    window = window_blocks * block_tokens
    window_start = (
        jnp.clip(where_gy - (window_blocks - 1), 0, count_gy - window_blocks) * block_tokens
    )
    key_rows = lax.dynamic_slice_in_dim(keys, window_start, window, 0)
    value_rows = lax.dynamic_slice_in_dim(values, window_start, window, 0)
    key_segment = lax.dynamic_slice_in_dim(segment_all, window_start, window, 0)
    key_index = window_start + jnp.arange(window, dtype=jnp.int32)
    allowed = (key_segment[None, :] == segment_own[:, None]) & (
        key_index[None, :] <= token_index[:, None]
    )
    score_scale = 1.0 / math.sqrt(HD)
    scores = (
        jnp.einsum("qhd,kd->hqk", queries, key_rows, preferred_element_type=jnp.float32)
        * score_scale
    )
    scores = jnp.where(allowed[None], scores, masked_out)
    row_max = jnp.max(scores, axis=2, keepdims=True)
    weights = jnp.where(allowed[None], jnp.exp(scores - row_max), 0.0)
    totals = jnp.sum(weights, axis=2)
    mixed = jnp.einsum(
        "hqk,kd->hqd", weights.astype(jnp.bfloat16), value_rows, preferred_element_type=jnp.float32
    )
    attention = (
        (mixed / totals[..., None])
        .astype(jnp.bfloat16)
        .transpose(1, 0, 2)
        .reshape(block_tokens, query_cols)
    )
    cache_cols = lax.dynamic_slice_in_dim(mine_all, first_query, block_tokens, 0)
    pages_dev = PAGES_DEV
    page_len = block_tokens // pages_dev
    page_range = jnp.arange(pages_dev, dtype=jnp.int32)
    width_cols = cache_cols.shape[1]
    my_pages = cache_cols.reshape(pages_dev, page_len * width_cols)
    capacity = max(1, pages_dev // count_gy)
    slots_all = count_gy * capacity
    owners = (cache_slot // pages_dev).reshape(count_gy, pages_dev)
    earlier = page_range[None, :] < page_range[:, None]
    same_owner = owners[:, :, None] == owners[:, None, :]
    ranks = jnp.sum((same_owner & earlier[None]).astype(jnp.int32), axis=2)
    my_owner = lax.dynamic_index_in_dim(owners, where_gy, 0, keepdims=False)
    my_rank = lax.dynamic_index_in_dim(ranks, where_gy, 0, keepdims=False)
    target = my_owner * capacity + my_rank
    slot_range = jnp.arange(slots_all, dtype=jnp.int32)
    send_map = (slot_range[:, None] == target[None, :]).astype(jnp.bfloat16)
    outgoing = jnp.dot(send_map, my_pages, preferred_element_type=jnp.float32).astype(jnp.bfloat16)
    incoming = lax.all_to_all(outgoing, "gy", split_axis=0, concat_axis=0, tiled=True)
    wanted = where_gy * pages_dev + page_range
    matches = cache_slot[None, :] == wanted[:, None]
    page_ids = jnp.arange(cache_slot.shape[0], dtype=jnp.int32)
    source_page = jnp.sum(jnp.where(matches, page_ids[None, :], 0), axis=1)
    source_rank = jnp.sum(jnp.where(matches, ranks.reshape(-1)[None, :], 0), axis=1)
    source_slot = source_page // pages_dev * capacity + source_rank
    take_map = (source_slot[:, None] == slot_range[None, :]).astype(jnp.bfloat16)
    cache_block = jnp.dot(take_map, incoming, preferred_element_type=jnp.float32)
    cache_block = cache_block.astype(jnp.bfloat16).reshape(pages_dev, page_len, width_cols)
    return (attention, cache_block)


def solution(mesh):
    return jax.shard_map(
        local,
        mesh=mesh,
        in_specs=(P("gx", "gy"), P("gy"), P("gx", "gy"), P(None, "gy"), P(), P()),
        out_specs=(P("gy", "gx"), P("gy", None, "gx")),
        check_vma=False,
    )
```

profile of v0, /device:TPU:2, one launch (start us, length us, event | category | flops | bytes accessed | tf_op | source)
XLA Modules:
  0.0 317.1 jit_solution(16310074648877330027)
XLA Ops:
  7.2 1.0 copy.44
  8.3 23.7 %all_to_all.22 = bf16[4,32,8,128]{3,2,0,1:T(8,128)(2,1)S(1)} all-to-all(bf16[4,32,8,128]{3,2,0,1:T(8,128)(2,1)S(1)} %copy.44), channel_id=1, replica_groups=mesh['gx'=8,'gy'=32] {'gy'}, dimensions={1} | all-to-all | bytes 524288 | tf_op jit(solution)/shard_map/all_to_all | solution.py:60
  32.0 0.7 copy.45
  32.8 1.6 pad_maximum_fusion.1
  34.5 36.5 %all-gather.1 = bf16[32,1,128]{2,1,0:T(2,128)(2,1)S(1)} all-gather(bf16[1,1,128]{2,1,0:T(2,128)(2,1)} %bitcast.75), channel_id=1, replica_groups=mesh['gx'=8,'gy'=32] {'gy'}, dimensions={0}, use_global_device_ids=true | all-gather | bytes 8448 | tf_op jit(solution)/shard_map/all_gather | solution.py:58
  71.0 0.8 reduce-window.8
  71.8 0.1 convert_reduce_fusion.2
  71.9 0.7 bitcast_subtract_fusion
  72.6 0.1 select_reduce_fusion
  72.7 2.1 multiply_reduce_fusion
  74.8 0.1 rsqrt.11
  74.9 4.1 %bitcast_convert_fusion = f32[8,4,32,8,128]{4,3,2,1,0:T(8,128)} fusion(bf16[32,32,8,128]{3,2,1,0:T(8,128)(2,1)} %all-gather.10.cloned.1.call-done), kind=kLoop, calls=%fused_computation.103 | loop fusion | flops 1048576 | bytes 6291456 | tf_op jit(solution)/shard_map/convert_element_type | solution.py:63
  79.0 67.4 %all-gather.6.cloned.1.call-done = bf16[640,4096]{1,0:T(8,128)(2,1)} async-done(((bf16[640,128]{1,0:T(8,128)(2,1)}), bf16[640,4096]{1,0:T(8,128)(2,1)}) %all-gather.6.cloned.1.call-update) | async-done | bytes 5242896 | tf_op jit(solution)/shard_map/all_gather | solution.py:57
  146.4 5.6 %fusion.8 = f32[256,640]{1,0:T(8,128)S(1)} fusion(bf16[640,4096]{1,0:T(8,128)(2,1)} %all-gather.6.cloned.1.call-done, f32[256,4096]{1,0:T(8,128)} %bitcast.62, f32[4096]{0:T(1024)S(1)} %bitcast.71, f32[256]{0:T(256)S(1)} %rsqrt.11), kind=kOutput, calls=%fused_computation.15 | convolution fusion | flops 1345323008 | bytes 10109952 | tf_op jit(solution)/shard_map/dot_general | solution.py:71
  152.0 0.6 fusion.37
  152.6 0.7 fusion.43
  153.4 0.1 convert_reduce_fusion
  153.5 0.1 dynamic_slice.25
  153.7 1.2 multiply_cosine_fusion
  154.9 77.7 %all-gather.8.cloned.1.call-done = bf16[32,32,8,128]{3,2,1,0:T(8,128)(2,1)} async-done(((bf16[1,32,8,128]{3,2,1,0:T(8,128)(2,1)}), bf16[32,32,8,128]{3,2,1,0:T(8,128)(2,1)}) %all-gather.8.cloned.1.call-update) | async-done | bytes 2097168 | tf_op jit(solution)/shard_map/all_gather | solution.py:84
  232.6 2.2 copy.46
  234.8 0.1 collective-permute-start
  234.9 4.4 %compare_and_fusion = pred[256,4352]{0,1:T(8,128)(4,1)} fusion(s32[256]{0:T(256)S(1)} %iota_add_fusion.1, s32[256]{0:T(256)S(1)} %dynamic_slice.26, s32[4352]{0:T(1024)S(1)} %iota_add_fusion, s32[4352]{0:T(1024)S(1)} %dynamic_slice.25), kind=kLoop, calls=%fused_computation.9 | loop fusion | flops 3342336 | bytes 1150976 | tf_op jit(solution)/shard_map/and | solution.py:103
  239.3 0.2 reshape.312
  239.5 1.4 subtract_convert_fusion
  240.9 0.4 pad_maximum_fusion
  241.3 0.8 convert_element_type.69
  242.1 5.6 %all-to-all-start.1 = ((bf16[32,8,512]{2,1,0:T(8,128)(2,1)}), bf16[32,8,512]{2,1,0:T(8,128)(2,1)S(1)}, u32[]{:S(2)}, u32[]{:S(2)}) async-start(bf16[32,8,512]{2,1,0:T(8,128)(2,1)} %convert_element_type.69), calls=%async_computation.1 | async-start | bytes 524288 | tf_op jit(solution)/shard_map/all_to_all | solution.py:81
  247.7 0.1 eq.103
  247.9 0.1 convert_reduce_fusion.1
  248.1 0.1 broadcast_in_dim.96
  248.1 0.2 add_reduce_fusion
  248.4 0.2 fusion.7
  248.6 0.5 broadcast.313
  249.1 0.7 reduce.4
  249.8 0.7 reshape.327
  250.5 9.8 %all-to-all-done.1 = bf16[32,8,512]{2,1,0:T(8,128)(2,1)S(1)} async-done(((bf16[32,8,512]{2,1,0:T(8,128)(2,1)}), bf16[32,8,512]{2,1,0:T(8,128)(2,1)S(1)}, u32[]{:S(2)}, u32[]{:S(2)}) %all-to-all-start.1) | async-done | bytes 262176 | tf_op jit(solution)/shard_map/all_to_all | solution.py:81
  260.3 5.1 %all-to-all-start.2 = ((bf16[32,2,1024]{2,1,0:T(2,128)(2,1)}), bf16[32,2,1024]{2,1,0:T(2,128)(2,1)S(1)}, u32[]{:S(2)}, u32[]{:S(2)}) async-start(bf16[32,2,1024]{2,1,0:T(2,128)(2,1)} %reshape.327), calls=%async_computation.2 | async-start | bytes 262144 | tf_op jit(solution)/shard_map/all_to_all | solution.py:142
  265.4 0.2 fusion.44
  265.6 0.8 reshape.313
  266.3 9.1 %all-to-all-done.2 = bf16[32,2,1024]{2,1,0:T(2,128)(2,1)S(1)} async-done(((bf16[32,2,1024]{2,1,0:T(2,128)(2,1)}), bf16[32,2,1024]{2,1,0:T(2,128)(2,1)S(1)}, u32[]{:S(2)}, u32[]{:S(2)}) %all-to-all-start.2) | async-done | bytes 131104 | tf_op jit(solution)/shard_map/all_to_all | solution.py:142
  275.5 0.1 reshape.328
  275.6 0.2 fusion.20
  275.8 0.6 copy.60
  276.4 10.0 %fusion.22 = f32[4352,256,4]{1,0,2:T(8,128)} fusion(pred[]{:T(512)S(6)} %eq.96, bf16[8192,128]{1,0:T(8,128)(2,1)} %collective-permute-done, s32[]{:T(128)S(6)} %select_n.101, bf16[8192,128]{1,0:T(8,128)(2,1)S(1)} %bitcast.66, bf16[256,4,128]{2,1,0:T(4,128)(2,1)} %reshape.313), kind=kOutput, calls=%fused_computation.23 | convolution fusion | flops 1141407744 | bytes 20316164 | tf_op jit(solution)/shard_map/qhd,kd->hqk/dot_general | solution.py:108
  286.4 18.1 %fusion.60 = (f32[4,256]{1,0:T(4,128)S(1)}, bf16[4,256,4352]{1,2,0:T(8,128)(2,1)}) fusion(f32[4352,256,4]{1,0,2:T(8,128)} %fusion.22, pred[256,4352]{0,1:T(8,128)(4,1)S(1)} %copy-done.1), kind=kOutput, calls=%fused_computation.107 | output fusion | flops 35655936 | bytes 27856896 | tf_op jit(solution)/shard_map/sub | solution.py:113
  304.5 5.3 %fusion.17 = bf16[256,4,128]{0,2,1:T(8,128)(2,1)S(1)} fusion(bf16[4,256,4352]{1,2,0:T(8,128)(2,1)} %get-tuple-element.23, pred[]{:T(512)S(6)} %eq.96, bf16[8192,128]{1,0:T(8,128)(2,1)} %collective-permute-done, s32[]{:T(128)S(6)} %select_n.101, bf16[8192,128]{1,0:T(8,128)(2,1)S(1)} %bitcast.67, f32[256,4]{0,1:T(4,128)S(1)} %bitcast.77), kind=kOutput, calls=%fused_computation.20 | convolution fusion | flops 1141669888 | bytes 11407365 | tf_op jit(solution)/shard_map/hqk,kd->hqd/dot_general | solution.py:115
  309.8 0.8 copy.55
  (33 shorter events, 0.6 us)
Async XLA Ops:
  7.2 25.7 %copy-start = (bf16[1024,128]{1,0:T(8,128)(2,1)S(1)}, bf16[1024,128]{1,0:T(8,128)(2,1)}, u32[]{:S(2)}) copy-start(bf16[1024,128]{1,0:T(8,128)(2,1)} %param.9) | copy-start | bytes 786436
  7.2 65.5 %all-gather.10.cloned.1.call-start = ((), (), s32[]{:S(2)}) async-start(), calls=%async_computation.5 | async-start | bytes 2359296 | tf_op jit(solution)/shard_map/all_gather | solution.py:61
  32.8 113.6 %all-gather.6.cloned.1.call-start = ((), (), s32[]{:S(2)}) async-start(), calls=%async_computation.3 | async-start | bytes 5406720 | tf_op jit(solution)/shard_map/all_gather | solution.py:57
  34.4 198.2 %all-gather.8.cloned.1.call-start = ((), (), s32[]{:S(2)}) async-start(), calls=%async_computation.4 | async-start | bytes 2162688 | tf_op jit(solution)/shard_map/all_gather | solution.py:84
  146.4 7.3 %copy-start.2 = (s32[512]{0:T(512)S(1)}, s32[512]{0:T(512)}, u32[]{:S(2)}) copy-start(s32[512]{0:T(512)} %param.11) | copy-start | bytes 6148
  234.8 41.6 %collective-permute-start = (bf16[8192,128]{1,0:T(8,128)(2,1)S(1)}, bf16[8192,128]{1,0:T(8,128)(2,1)}, u32[]{:S(2)}, u32[]{:S(2)}) collective-permute-start(bf16[8192,128]{1,0:T(8,128)(2,1)S(1)} %bitcast.64), channel_id=1, source_target_pairs={{0,32},{32,0},{64,96},{96,64},{128,160},{160,128},{192,224},{224,1... | collective-permute-start | bytes 6291464 | tf_op jit(solution)/shard_map/ppermute | solution.py:86
  242.1 18.1 %all-to-all-start.1 = ((bf16[32,8,512]{2,1,0:T(8,128)(2,1)}), bf16[32,8,512]{2,1,0:T(8,128)(2,1)S(1)}, u32[]{:S(2)}, u32[]{:S(2)}) async-start(bf16[32,8,512]{2,1,0:T(8,128)(2,1)} %convert_element_type.69), calls=%async_computation.1 | async-start | bytes 524288 | tf_op jit(solution)/shard_map/all_to_all | solution.py:81
  260.3 15.2 %all-to-all-start.2 = ((bf16[32,2,1024]{2,1,0:T(2,128)(2,1)}), bf16[32,2,1024]{2,1,0:T(2,128)(2,1)S(1)}, u32[]{:S(2)}, u32[]{:S(2)}) async-start(bf16[32,2,1024]{2,1,0:T(2,128)(2,1)} %reshape.327), calls=%async_computation.2 | async-start | bytes 262144 | tf_op jit(solution)/shard_map/all_to_all | solution.py:142
  276.4 10.0 %copy-start.1 = (pred[256,4352]{0,1:T(8,128)(4,1)S(1)}, pred[256,4352]{0,1:T(8,128)(4,1)}, u32[]{:S(2)}) copy-start(pred[256,4352]{0,1:T(8,128)(4,1)} %compare_and_fusion) | copy-start | bytes 3342340
Sparse Core Ops, SparseCore 0:
  32.9 22.5 all-gather.9
  57.9 88.4 all-gather.5
  153.5 79.0 all-gather.7
where the time goes:
time: 318 us; the launch traced here: 317 us
  waiting for transfers between devices  164 us (52%)
  blocking collectives  60.2 us (19%)
  other arithmetic  37.6 us (12%)
  matrix products  21.2 us (7%)
  between operations  14 us (4%)
  starting transfers between devices  10.9 us (3%)
  local copies, waits for them, and re-layouts  9.22 us (3%)
    all_gather x1, waiting for transfers between devices, local(): lax.all_gather(mine.reshape(count_gy, sub, HD), 'gy', axis=0, tiled=False)  77.7 us
    all_gather x1, waiting for transfers between devices, local(): weights_full = lax.all_gather(stacked, 'gy', axis=1, tiled=True)  67.4 us
    all_gather x1, blocking collectives, local(): gain_full = lax.all_gather(norm_gain, 'gy', axis=0, tiled=True)  36.5 us
    all_to_all x1, blocking collectives, local(): pieces = lax.all_to_all(pieces, 'gy', 1, 1, tiled=True)  23.7 us
    sub x1, other arithmetic, local(): weights = jnp.where(allowed[None], jnp.exp(scores - row_max), 0.0)  18.1 us
    dot_general x1, matrix products, local(): jnp.einsum('qhd,kd->hqk', queries, key_rows, preferred_element_type=jnp.f...  9.99 us
    all_to_all x1, waiting for transfers between devices, local(): lax.all_to_all(queries.reshape(count_gy, sub, query_cols), 'gy', 0, 0, ti...  9.77 us
    all_to_all x1, waiting for transfers between devices, local(): lax.all_to_all(outgoing, 'gy', split_axis=0, concat_axis=0, tiled=True)  9.12 us
  transfers between devices with their start and end apart: 6, of which 4 were waited for; matrix products, arithmetic and copies ran while one was open for 7% of the time, Pallas kernels for 0%

commit v1 on v0

--- a/solution.py
+++ b/solution.py
@@ -13,6 +13,11 @@
 epsilon = 1e-06
 rope_base = 5000000.0
 masked_out = -1e30
+
+
+def gather_from_all(shard, axis, dim):
+    copies = jnp.concatenate([shard] * lax.axis_size(axis), axis=dim)
+    return lax.all_to_all(copies, axis, dim, dim, tiled=True)
 
 
 def token_places(prompt_lengths, token_index):
@@ -55,7 +60,7 @@
     kv_rows = lax.dynamic_slice_in_dim(kv_proj, where_gx * HD, HD, 0)
     stacked = jnp.concatenate([query_proj, kv_rows], axis=0)
     weights_full = lax.all_gather(stacked, "gy", axis=1, tiled=True)
-    gain_full = lax.all_gather(norm_gain, "gy", axis=0, tiled=True)
+    gain_full = gather_from_all(norm_gain, "gy", 0)
     pieces = hidden_in.reshape(blocks_per_slab, count_gy, sub, local_feats)
     pieces = lax.all_to_all(pieces, "gy", 1, 1, tiled=True)
     rows_here = lax.all_gather(pieces, "gx", axis=0, tiled=False)

time: 318 us -> 318 us (level)
  blocking collectives: 60.2 us -> 23.7 us
  waiting for transfers between devices: 164 us -> 195 us
  starting transfers between devices: 10.9 us -> 15.3 us
    all_gather x1 -> x0, blocking collectives: 36.5 us -> none  [local(): gain_full = lax.all_gather(norm_gain, 'gy', axis=0, tiled=True)]
    all_gather x1, waiting for transfers between devices: 67.4 us -> 84.9 us  [local(): weights_full = lax.all_gather(stacked, 'gy', axis=1, tiled=True)]
    all_to_all x0 -> x1, waiting for transfers between devices: none -> 7.99 us  [gather_from_all(): return lax.all_to_all(copies, axis, dim, dim, tiled=True)]
    all_gather x1, waiting for transfers between devices: 0.01 us -> 5.29 us  [local(): rows_here = lax.all_gather(pieces, 'gx', axis=0, tiled=False)]
    all_to_all x0 -> x1, starting transfers between devices: none -> 4.4 us  [gather_from_all(): return lax.all_to_all(copies, axis, dim, dim, tiled=True)]
  transfers between devices with their start and end apart: 6 -> 7, of which waited for: 4 -> 6; matrix products, arithmetic and copies ran while one was open for 7% -> 8% of each run, Pallas kernels for 0% -> 0%
where the time goes in v1:
time: 318 us; the launch traced here: 317 us
  waiting for transfers between devices  195 us (61%)
  other arithmetic  37.6 us (12%)
  blocking collectives  23.7 us (7%)
  matrix products  21.2 us (7%)
  starting transfers between devices  15.3 us (5%)
  between operations  14 us (4%)
  local copies, waits for them, and re-layouts  10.5 us (3%)
    all_gather x1, waiting for transfers between devices, local(): weights_full = lax.all_gather(stacked, 'gy', axis=1, tiled=True)  84.9 us
    all_gather x1, waiting for transfers between devices, local(): lax.all_gather(mine.reshape(count_gy, sub, HD), 'gy', axis=0, tiled=False)  77.7 us
    all_to_all x1, blocking collectives, local(): pieces = lax.all_to_all(pieces, 'gy', 1, 1, tiled=True)  23.7 us
    sub x1, other arithmetic, local(): weights = jnp.where(allowed[None], jnp.exp(scores - row_max), 0.0)  18.1 us
    dot_general x1, matrix products, local(): jnp.einsum('qhd,kd->hqk', queries, key_rows, preferred_element_type=jnp.f...  9.99 us
    all_to_all x1, waiting for transfers between devices, local(): lax.all_to_all(queries.reshape(count_gy, sub, query_cols), 'gy', 0, 0, ti...  9.77 us
    all_to_all x1, waiting for transfers between devices, local(): lax.all_to_all(outgoing, 'gy', split_axis=0, concat_axis=0, tiled=True)  9.12 us
    all_to_all x1, waiting for transfers between devices, gather_from_all(): return lax.all_to_all(copies, axis, dim, dim, tiled=True)  7.99 us
  transfers between devices with their start and end apart: 7, of which 6 were waited for; matrix products, arithmetic and copies ran while one was open for 8% of the time, Pallas kernels for 0%

profile of v1, /device:TPU:2, one launch (start us, length us, event | category | flops | bytes accessed | tf_op | source)
XLA Modules:
  0.0 317.1 jit_solution(10395400145333613642)
XLA Ops:
  7.2 1.0 copy.47
  8.3 23.7 %all_to_all.28 = bf16[4,32,8,128]{3,2,0,1:T(8,128)(2,1)S(1)} all-to-all(bf16[4,32,8,128]{3,2,0,1:T(8,128)(2,1)S(1)} %copy.47), channel_id=1, replica_groups=mesh['gx'=8,'gy'=32] {'gy'}, dimensions={1} | all-to-all | bytes 524288 | tf_op jit(solution)/shard_map/all_to_all | solution.py:65
  32.0 0.7 copy.48
  32.8 1.6 pad_maximum_fusion.1
  34.4 1.3 concatenate.14
  35.7 4.4 %all-to-all-start.1 = ((bf16[32,128,1]{1,2,0:T(2,128)(2,1)}), bf16[32,128,1]{1,2,0:T(2,128)(2,1)S(1)}, u32[]{:S(2)}, u32[]{:S(2)}) async-start(bf16[32,128,1]{1,2,0:T(2,128)(2,1)} %concatenate.14), calls=%async_computation.1 | async-start | bytes 32768 | tf_op jit(solution)/shard_map/all_to_all | solution.py:20
  40.2 0.8 reduce-window.8
  41.0 0.1 convert_reduce_fusion.2
  41.1 0.7 bitcast_subtract_fusion
  41.8 0.1 select_reduce_fusion
  41.9 8.0 %all-to-all-done.1 = bf16[32,128,1]{1,2,0:T(2,128)(2,1)S(1)} async-done(((bf16[32,128,1]{1,2,0:T(2,128)(2,1)}), bf16[32,128,1]{1,2,0:T(2,128)(2,1)S(1)}, u32[]{:S(2)}, u32[]{:S(2)}) %all-to-all-start.1) | async-done | bytes 8224 | tf_op jit(solution)/shard_map/all_to_all | solution.py:20
  49.9 5.3 %all-gather.9.cloned.1.call-done = bf16[32,32,8,128]{3,2,1,0:T(8,128)(2,1)} async-done(((bf16[4,32,8,128]{3,2,1,0:T(8,128)(2,1)}), bf16[32,32,8,128]{3,2,1,0:T(8,128)(2,1)}) %all-gather.9.cloned.1.call-update) | async-done | bytes 2097168 | tf_op jit(solution)/shard_map/all_gather | solution.py:66
  55.2 2.1 multiply_reduce_fusion
  57.3 0.1 rsqrt.11
  57.4 4.1 %bitcast_convert_fusion.1 = f32[8,4,32,8,128]{4,3,2,1,0:T(8,128)} fusion(bf16[32,32,8,128]{3,2,1,0:T(8,128)(2,1)} %all-gather.9.cloned.1.call-done), kind=kLoop, calls=%fused_computation.104 | loop fusion | flops 1048576 | bytes 6291456 | tf_op jit(solution)/shard_map/convert_element_type | solution.py:68
  61.5 84.9 %all-gather.5.cloned.1.call-done = bf16[640,4096]{1,0:T(8,128)(2,1)} async-done(((bf16[640,128]{1,0:T(8,128)(2,1)}), bf16[640,4096]{1,0:T(8,128)(2,1)}) %all-gather.5.cloned.1.call-update) | async-done | bytes 5242896 | tf_op jit(solution)/shard_map/all_gather | solution.py:62
  146.4 5.6 %fusion.8 = f32[256,640]{1,0:T(8,128)S(1)} fusion(bf16[640,4096]{1,0:T(8,128)(2,1)} %all-gather.5.cloned.1.call-done, f32[256,4096]{1,0:T(8,128)} %bitcast.63, f32[4096]{0:T(1024)S(1)} %bitcast_convert_fusion, f32[256]{0:T(256)S(1)} %rsqrt.11), kind=kOutput, calls=%fused_computation.15 | convolution fusion | flops 1345323008 | bytes 10109952 | tf_op jit(solution)/shard_map/dot_general | solution.py:76
  152.0 0.6 fusion.37
  152.6 0.7 fusion.43
  153.4 0.1 convert_reduce_fusion
  153.7 1.2 multiply_cosine_fusion
  155.0 77.7 %all-gather.7.cloned.1.call-done = bf16[32,32,8,128]{3,2,1,0:T(8,128)(2,1)} async-done(((bf16[1,32,8,128]{3,2,1,0:T(8,128)(2,1)}), bf16[32,32,8,128]{3,2,1,0:T(8,128)(2,1)}) %all-gather.7.cloned.1.call-update) | async-done | bytes 2097168 | tf_op jit(solution)/shard_map/all_gather | solution.py:89
  232.6 2.2 copy.50
  234.8 0.1 collective-permute-start
  234.9 4.4 %compare_and_fusion = pred[256,4352]{0,1:T(8,128)(4,1)} fusion(s32[256]{0:T(256)S(1)} %iota_add_fusion.1, s32[256]{0:T(256)S(1)} %dynamic_slice.26, s32[4352]{0:T(1024)S(1)} %iota_add_fusion, s32[4352]{0:T(1024)S(1)} %dynamic_slice.25), kind=kLoop, calls=%fused_computation.9 | loop fusion | flops 3342336 | bytes 1150976 | tf_op jit(solution)/shard_map/and | solution.py:108
  239.3 0.2 reshape.354
  239.5 1.4 subtract_convert_fusion
  240.9 0.4 pad_maximum_fusion
  241.3 0.8 convert_element_type.77
  242.1 5.6 %all-to-all-start.2 = ((bf16[32,8,512]{2,1,0:T(8,128)(2,1)}), bf16[32,8,512]{2,1,0:T(8,128)(2,1)S(1)}, u32[]{:S(2)}, u32[]{:S(2)}) async-start(bf16[32,8,512]{2,1,0:T(8,128)(2,1)} %convert_element_type.77), calls=%async_computation.2 | async-start | bytes 524288 | tf_op jit(solution)/shard_map/all_to_all | solution.py:86
  247.9 0.1 convert_reduce_fusion.1
  248.2 0.2 add_reduce_fusion
  248.4 0.2 fusion.7
  248.6 0.5 broadcast.314
  249.1 0.7 reduce.4
  249.8 0.7 reshape.367
  250.5 9.8 %all-to-all-done.2 = bf16[32,8,512]{2,1,0:T(8,128)(2,1)S(1)} async-done(((bf16[32,8,512]{2,1,0:T(8,128)(2,1)}), bf16[32,8,512]{2,1,0:T(8,128)(2,1)S(1)}, u32[]{:S(2)}, u32[]{:S(2)}) %all-to-all-start.2) | async-done | bytes 262176 | tf_op jit(solution)/shard_map/all_to_all | solution.py:86
  260.3 5.1 %all-to-all-start.3 = ((bf16[32,2,1024]{2,1,0:T(2,128)(2,1)}), bf16[32,2,1024]{2,1,0:T(2,128)(2,1)S(1)}, u32[]{:S(2)}, u32[]{:S(2)}) async-start(bf16[32,2,1024]{2,1,0:T(2,128)(2,1)} %reshape.367), calls=%async_computation.3 | async-start | bytes 262144 | tf_op jit(solution)/shard_map/all_to_all | solution.py:147
  265.4 0.2 fusion.44
  265.6 0.8 reshape.355
  266.3 9.1 %all-to-all-done.3 = bf16[32,2,1024]{2,1,0:T(2,128)(2,1)S(1)} async-done(((bf16[32,2,1024]{2,1,0:T(2,128)(2,1)}), bf16[32,2,1024]{2,1,0:T(2,128)(2,1)S(1)}, u32[]{:S(2)}, u32[]{:S(2)}) %all-to-all-start.3) | async-done | bytes 131104 | tf_op jit(solution)/shard_map/all_to_all | solution.py:147
  275.5 0.1 reshape.368
  275.6 0.2 fusion.20
  275.8 0.6 copy.64
  276.4 10.0 %fusion.22 = f32[4352,256,4]{1,0,2:T(8,128)} fusion(pred[]{:T(512)S(6)} %eq.96, bf16[8192,128]{1,0:T(8,128)(2,1)} %collective-permute-done, s32[]{:T(128)S(6)} %select_n.101, bf16[8192,128]{1,0:T(8,128)(2,1)S(1)} %bitcast.67, bf16[256,4,128]{2,1,0:T(4,128)(2,1)} %reshape.355), kind=kOutput, calls=%fused_computation.23 | convolution fusion | flops 1141407744 | bytes 20316164 | tf_op jit(solution)/shard_map/qhd,kd->hqk/dot_general | solution.py:113
  286.4 18.1 %fusion.60 = (f32[4,256]{1,0:T(4,128)S(1)}, bf16[4,256,4352]{1,2,0:T(8,128)(2,1)}) fusion(f32[4352,256,4]{1,0,2:T(8,128)} %fusion.22, pred[256,4352]{0,1:T(8,128)(4,1)S(1)} %copy-done.1), kind=kOutput, calls=%fused_computation.108 | output fusion | flops 35655936 | bytes 27856896 | tf_op jit(solution)/shard_map/sub | solution.py:118
  304.5 5.3 %fusion.17 = bf16[256,4,128]{0,2,1:T(8,128)(2,1)S(1)} fusion(bf16[4,256,4352]{1,2,0:T(8,128)(2,1)} %get-tuple-element.23, pred[]{:T(512)S(6)} %eq.96, bf16[8192,128]{1,0:T(8,128)(2,1)} %collective-permute-done, s32[]{:T(128)S(6)} %select_n.101, bf16[8192,128]{1,0:T(8,128)(2,1)S(1)} %bitcast.68, f32[256,4]{0,1:T(4,128)S(1)} %bitcast.76), kind=kOutput, calls=%fused_computation.20 | convolution fusion | flops 1141669888 | bytes 11407365 | tf_op jit(solution)/shard_map/hqk,kd->hqd/dot_general | solution.py:120
  309.8 0.8 copy.59
  (35 shorter events, 0.9 us)
Async XLA Ops:
  7.2 25.7 %copy-start = (bf16[1024,128]{1,0:T(8,128)(2,1)S(1)}, bf16[1024,128]{1,0:T(8,128)(2,1)}, u32[]{:S(2)}) copy-start(bf16[1024,128]{1,0:T(8,128)(2,1)} %param.9) | copy-start | bytes 786436
  7.2 48.0 %all-gather.9.cloned.1.call-start = ((), (), s32[]{:S(2)}) async-start(), calls=%async_computation.6 | async-start | bytes 2359296 | tf_op jit(solution)/shard_map/all_gather | solution.py:66
  32.8 113.6 %all-gather.5.cloned.1.call-start = ((), (), s32[]{:S(2)}) async-start(), calls=%async_computation.4 | async-start | bytes 5406720 | tf_op jit(solution)/shard_map/all_gather | solution.py:62
  35.7 14.2 %all-to-all-start.1 = ((bf16[32,128,1]{1,2,0:T(2,128)(2,1)}), bf16[32,128,1]{1,2,0:T(2,128)(2,1)S(1)}, u32[]{:S(2)}, u32[]{:S(2)}) async-start(bf16[32,128,1]{1,2,0:T(2,128)(2,1)} %concatenate.14), calls=%async_computation.1 | async-start | bytes 32768 | tf_op jit(solution)/shard_map/all_to_all | solution.py:20
  40.1 192.5 %all-gather.7.cloned.1.call-start = ((), (), s32[]{:S(2)}) async-start(), calls=%async_computation.5 | async-start | bytes 2162688 | tf_op jit(solution)/shard_map/all_gather | solution.py:89
  146.4 7.3 %copy-start.2 = (s32[512]{0:T(512)S(1)}, s32[512]{0:T(512)}, u32[]{:S(2)}) copy-start(s32[512]{0:T(512)} %param.11) | copy-start | bytes 6148
  234.8 41.6 %collective-permute-start = (bf16[8192,128]{1,0:T(8,128)(2,1)S(1)}, bf16[8192,128]{1,0:T(8,128)(2,1)}, u32[]{:S(2)}, u32[]{:S(2)}) collective-permute-start(bf16[8192,128]{1,0:T(8,128)(2,1)S(1)} %bitcast.65), channel_id=1, source_target_pairs={{0,32},{32,0},{64,96},{96,64},{128,160},{160,128},{192,224},{224,1... | collective-permute-start | bytes 6291464 | tf_op jit(solution)/shard_map/ppermute | solution.py:91
  242.1 18.1 %all-to-all-start.2 = ((bf16[32,8,512]{2,1,0:T(8,128)(2,1)}), bf16[32,8,512]{2,1,0:T(8,128)(2,1)S(1)}, u32[]{:S(2)}, u32[]{:S(2)}) async-start(bf16[32,8,512]{2,1,0:T(8,128)(2,1)} %convert_element_type.77), calls=%async_computation.2 | async-start | bytes 524288 | tf_op jit(solution)/shard_map/all_to_all | solution.py:86
  260.3 15.2 %all-to-all-start.3 = ((bf16[32,2,1024]{2,1,0:T(2,128)(2,1)}), bf16[32,2,1024]{2,1,0:T(2,128)(2,1)S(1)}, u32[]{:S(2)}, u32[]{:S(2)}) async-start(bf16[32,2,1024]{2,1,0:T(2,128)(2,1)} %reshape.367), calls=%async_computation.3 | async-start | bytes 262144 | tf_op jit(solution)/shard_map/all_to_all | solution.py:147
  276.4 10.0 %copy-start.1 = (pred[256,4352]{0,1:T(8,128)(4,1)S(1)}, pred[256,4352]{0,1:T(8,128)(4,1)}, u32[]{:S(2)}) copy-start(pred[256,4352]{0,1:T(8,128)(4,1)} %compare_and_fusion) | copy-start | bytes 3342340
Sparse Core Ops, SparseCore 0:
  32.9 22.2 all-gather.8
  57.6 88.7 all-gather.4
  153.5 79.0 all-gather.6
